TPU v7x, 32 devices: a whole 2x2x4 slice. The times are simulated.
32 devices in a mesh: grp: 2 (over x), blk: 2 (over core), head: 8 (over z, y).
Axes of the slice: x: 2, y: 2, z: 4, core: 2. Of those that a mesh axis runs over, the one named last changes fastest.
Arguments:
- stream: bfloat16 [1024, 3072], P(('grp', 'blk', 'head')), parts along dimension 0, may hold values from -6 to 6
- gains: float32 [3, 3072], replicated, may hold values from 0.25 to 1.75
- dilations: int32 [2], replicated, may hold values from 1 to 64, as said below
- w_conv: bfloat16 [2, 3, 3072, 2, 3072], P(None, None, None, None, 'head'), may hold values from -0.0625 to 0.0625
- w_mix: bfloat16 [2, 3072, 3072], P(None, 'head'), may hold values from -0.109375 to 0.109375
- w_qkv: bfloat16 [3072, 3, 8, 128], P(None, None, 'head')
- w_out: bfloat16 [8, 128, 3072], P('head'), may hold values from -0.1875 to 0.1875
Outputs:
- mixed: bfloat16 [1024, 3072], P(('grp', 'blk', 'head')), parts along dimension 0
There are 2 independent parts, one for each index of `grp`. A program takes and returns all parts, laid end to end along the dimension named above; an argument that names none is the same for every part. Nothing has to cross between parts.
Inputs may be any that keep to these rules, and one draw needn't show every extreme that they name: `dilations`: each dilation is a whole number; one is exactly 64.
All inputs are finite; a program needn't handle non-finite values.
Results may differ from a plain program's by a relative error of at most 0.03.
Values may be sent and summed in bfloat16 or wider, within the bound.
No kernel may reach another device: no remote copies, remote signals or barrier semaphores. Data moves between devices by JAX's collectives and lax.ppermute only.
A program may use at most 128 MiB of HBM per device.

v0:
```python
import jax
import jax.numpy as jnp
from jax import lax
from jax.sharding import PartitionSpec as P

LARGEST_DILATION = 64


def shifted(value, axis, by):
    length = lax.axis_size(axis)
    pairs = [(i, i + by) for i in range(length) if 0 <= i + by < length]
    return lax.ppermute(value, axis, pairs)


def normed(values, gain):
    wide = values.astype(jnp.float32)
    scale = lax.rsqrt(jnp.mean(wide * wide, axis=-1, keepdims=True) + 1e-06)
    return (wide * scale * gain).astype(jnp.bfloat16)


def rounded_term(left, right):
    term = jnp.dot(left, right, preferred_element_type=jnp.float32)
    return lax.optimization_barrier(term.astype(jnp.bfloat16)).astype(jnp.float32)


def convolution_gate(hidden, kernel, dilation_factor):
    all_rows = hidden.shape[0]
    width = hidden.shape[1]
    own_width = kernel.shape[-1]
    border_rows = 2 * LARGEST_DILATION
    before = shifted(hidden[all_rows - border_rows :], "blk", 1)
    padded = jnp.concatenate([before, hidden], axis=0)
    pre_act = jnp.zeros((all_rows, 2 * own_width), jnp.float32)
    for tap_idx in range(3):
        start = border_rows - tap_idx * dilation_factor
        slab = lax.dynamic_slice_in_dim(padded, start, all_rows, 0)
        pre_act = pre_act + jnp.dot(
            slab, kernel[tap_idx].reshape(width, 2 * own_width), preferred_element_type=jnp.float32
        )
    return (jnp.tanh(pre_act[:, :own_width]) * jax.nn.sigmoid(pre_act[:, own_width:])).astype(
        jnp.bfloat16
    )


def conv_share(gated, weight, tok_rows):

    def term(start, count):
        return rounded_term(gated, weight)

    return lax.psum_scatter(
        term(jnp.int32(0), tok_rows * lax.axis_size("head")).astype(jnp.bfloat16),
        "head",
        scatter_dimension=0,
        tiled=True,
    ).astype(jnp.float32)


def attention_portion_for(heads_out, out_block, tok_rows):

    def term(start, count):
        return rounded_term(heads_out, out_block)

    return lax.psum_scatter(
        term(jnp.int32(0), tok_rows * lax.axis_size("head")).astype(jnp.bfloat16),
        "head",
        scatter_dimension=0,
        tiled=True,
    ).astype(jnp.float32)


def attend(queries, keys_in, values_in, causal):
    scale = queries.shape[1] ** (-0.5)
    scores = jnp.einsum("qd,kd->qk", queries, keys_in, preferred_element_type=jnp.float32) * scale
    if causal:
        rows_q = lax.broadcasted_iota(jnp.int32, scores.shape, 0)
        rows_k = lax.broadcasted_iota(jnp.int32, scores.shape, 1)
        scores = jnp.where(rows_q >= rows_k, scores, -1e30)
    peak = jnp.max(scores, axis=1)
    probs = jnp.exp(scores - peak[:, None])
    denom = jnp.sum(probs, axis=1)
    weighted = jnp.dot(probs.astype(jnp.bfloat16), values_in, preferred_element_type=jnp.float32)
    return (peak, denom, weighted)


def neutral(count, head_size):
    return (
        jnp.full((count,), -1e30, jnp.float32),
        jnp.zeros((count,), jnp.float32),
        jnp.zeros((count, head_size), jnp.float32),
    )


def combine(first, second):
    peak = jnp.maximum(first[0], second[0])
    scale_one = jnp.exp(first[0] - peak)
    scale_two = jnp.exp(second[0] - peak)
    denom = first[1] * scale_one + second[1] * scale_two
    weighted = first[2] * scale_one[:, None] + second[2] * scale_two[:, None]
    return (peak, denom, weighted)


def per_device(stream, gains, dilations, w_conv, w_mix, w_qkv, w_out):
    blk_pos = lax.axis_index("blk")
    tok_rows = stream.shape[0]
    width = stream.shape[1]
    head_size = w_qkv.shape[3]
    layers = w_conv.shape[0]
    qkv_weight = w_qkv.reshape(width, 3 * head_size)
    share = stream
    state = lax.all_gather(stream, "head", axis=0, tiled=True)
    for layer_idx in range(layers):
        gated = convolution_gate(
            normed(state, gains[layer_idx]), w_conv[layer_idx], dilations[layer_idx]
        )
        summed = conv_share(gated, w_mix[layer_idx], tok_rows)
        share = (share.astype(jnp.float32) + summed).astype(jnp.bfloat16)
        state = lax.all_gather(share, "head", axis=0, tiled=True)
    all_rows = state.shape[0]
    attn_in = normed(state, gains[layers])
    projected = jnp.dot(attn_in, qkv_weight, preferred_element_type=jnp.float32).astype(
        jnp.bfloat16
    )
    queries = projected[:, :head_size]
    keys_own = projected[:, head_size : 2 * head_size]
    values_own = projected[:, 2 * head_size :]
    keys_prev, values_prev = shifted((keys_own, values_own), "blk", 1)
    own_part = attend(queries, keys_own, values_own, True)
    crossing_portion = lax.cond(
        blk_pos > 0,
        lambda: attend(queries, keys_prev, values_prev, False),
        lambda: neutral(all_rows, head_size),
    )
    peak, denom, weighted = combine(own_part, crossing_portion)
    heads_out = (weighted / denom[:, None]).astype(jnp.bfloat16)
    attn_share = attention_portion_for(heads_out, w_out[0], tok_rows)
    return (share.astype(jnp.float32) + attn_share).astype(jnp.bfloat16)


def solution(mesh):
    placed = (
        P(("grp", "blk", "head"), None),
        P(),
        P(),
        P(None, None, None, None, "head"),
        P(None, "head", None),
        P(None, None, "head", None),
        P("head", None, None),
    )
    return jax.shard_map(
        per_device,
        mesh=mesh,
        in_specs=placed,
        out_specs=P(("grp", "blk", "head"), None),
        check_vma=False,
    )
```

profile of v0, /device:TPU:0, one launch (start us, length us, event | category | flops | bytes accessed | tf_op | source)
XLA Modules:
  0.0 449.6 jit_solution(16338248343998651655)
XLA Ops:
  6.5 0.7 all-gather.4.cloned.1.call-update
  7.3 0.9 fusion.97
  8.3 48.2 %all-gather.4.cloned.1.call-done = bf16[256,3072]{1,0:T(8,128)(2,1)} async-done(((bf16[32,3072]{1,0:T(8,128)(2,1)}), bf16[256,3072]{1,0:T(8,128)(2,1)}) %all-gather.4.cloned.1.call-update) | async-done | bytes 1572880 | tf_op jit(solution)/shard_map/all_gather | solution.py:110
  56.5 1.8 fusion.5
  58.3 1.9 fusion.7
  60.2 0.1 slice.102
  60.3 2.2 collective-permute-start
  62.4 22.4 %fusion.95 = (bf16[1,1,3072,2,384]{4,3,2,1,0:T(2,128)(2,1)}, bf16[1,1,3072,2,384]{4,3,2,1,0:T(2,128)(2,1)}, bf16[1,1,3072,2,384]{4,3,2,1,0:T(2,128)(2,1)S(1)}, b...) fusion(bf16[2,3,3072,2,384]{4,3,2,1,0:T(2,128)(2,1)} %param.12), kind=kLoop, calls=%fused_computation.106 | loop fusion | bytes 56623104 | tf_op jit(solution)/shard_map/slice | solution.py:38
  84.8 0.7 fusion.98
  87.4 3.0 copy.11
  90.4 3.0 copy.9
  93.4 3.1 copy.10
  96.5 3.9 fusion.100
  100.4 4.4 fusion.25
  104.9 2.9 fusion.37
  107.8 2.2 convolution_convert_fusion.2
  110.0 0.0 all-gather.6.cloned.1.call-start
  110.1 64.3 %reduce-scatter.4.cloned.1.call-done = bf16[32,3072]{1,0:T(8,128)(2,1)} async-done(((bf16[256,3072]{1,0:T(8,128)(2,1)}), bf16[32,3072]{1,0:T(8,128)(2,1)}) %reduce-scatter.4.cloned.1.call-update) | async-done | bytes 196624 | tf_op jit(solution)/shard_map/reduce_scatter | solution.py:50
  174.4 1.6 add_convert_fusion.2
  176.1 43.9 %all-gather.6.cloned.1.call-done = bf16[256,3072]{1,0:T(8,128)(2,1)} async-done(((bf16[32,3072]{1,0:T(8,128)(2,1)}), bf16[256,3072]{1,0:T(8,128)(2,1)}) %all-gather.6.cloned.1.call-update) | async-done | bytes 1572880 | tf_op jit(solution)/shard_map/all_gather | solution.py:117
  220.0 1.8 fusion.8
  221.8 1.9 fusion.10
  223.7 0.1 slice.105
  223.7 2.2 collective-permute-start.1
  227.8 5.3 %copy.14 = bf16[384,8,2,384]{3,1,2,0:T(8,128)(2,1)} copy(bf16[384,8,2,384]{3,2,1,0:T(2,128)(2,1)} %bitcast.55) | data formatting | bytes 9437184
  233.1 5.5 %copy.12 = bf16[384,8,2,384]{3,1,2,0:T(8,128)(2,1)} copy(bf16[384,8,2,384]{3,2,1,0:T(2,128)(2,1)} %bitcast.54) | data formatting | bytes 9437184
  238.6 3.0 copy.13
  241.7 3.9 fusion.101
  245.6 2.9 fusion.19
  248.5 2.7 fusion.43
  251.2 2.2 convolution_convert_fusion.1
  253.5 64.3 %reduce-scatter.6.cloned.1.call-done = bf16[32,3072]{1,0:T(8,128)(2,1)} async-done(((bf16[256,3072]{1,0:T(8,128)(2,1)}), bf16[32,3072]{1,0:T(8,128)(2,1)}) %reduce-scatter.6.cloned.1.call-update) | async-done | bytes 196624 | tf_op jit(solution)/shard_map/reduce_scatter | solution.py:50
  317.8 1.6 add_convert_fusion.1
  319.6 2.5 copy.8
  322.1 40.9 %all-gather.8.cloned.1.call-done = bf16[256,3072]{1,0:T(8,128)(2,1)} async-done(((bf16[32,3072]{1,0:T(8,128)(2,1)}), bf16[256,3072]{1,0:T(8,128)(2,1)}) %all-gather.8.cloned.1.call-update) | async-done | bytes 1572880 | tf_op jit(solution)/shard_map/all_gather | solution.py:117
  363.0 1.8 fusion.11
  364.8 3.2 fusion.46
  368.0 0.2 fusion.99
  368.2 1.3 collective-permute-start.2
  369.5 1.3 collective-permute-start.3
  370.8 0.1 fusion.61
  370.9 0.8 collective-permute-done.3
  371.7 0.6 conditional.1
  371.7 0.6 broadcast.54
  372.3 0.7 multiply_add_fusion
  373.0 1.9 convolution_convert_fusion
  375.0 66.2 %reduce-scatter.8.cloned.1.call-done = bf16[32,3072]{1,0:T(8,128)(2,1)} async-done(((bf16[256,3072]{1,0:T(8,128)(2,1)}), bf16[32,3072]{1,0:T(8,128)(2,1)}) %reduce-scatter.8.cloned.1.call-update) | async-done | bytes 196624 | tf_op jit(solution)/shard_map/reduce_scatter | solution.py:63
  441.1 1.6 add_convert_fusion
  (58 shorter events, 0.4 us)
Async XLA Ops:
  6.5 366.5 %copy-start = (bf16[1,128,3072]{2,1,0:T(8,128)(2,1)S(1)}, bf16[1,128,3072]{2,1,0:T(8,128)(2,1)}, u32[]{:S(2)}) copy-start(bf16[1,128,3072]{2,1,0:T(8,128)(2,1)} %param.15) | copy-start | bytes 2359300
  6.5 49.9 %all-gather.4.cloned.1.call-start = ((), (), s32[]{:S(2)}) async-start(), calls=%async_computation.3 | async-start | bytes 1769472 | tf_op jit(solution)/shard_map/all_gather | solution.py:110
  7.3 167.1 %reduce-scatter.4.cloned.1.call-start = ((), (), s32[]{:S(2)}) async-start(), calls=%async_computation.4 | async-start | bytes 1769472 | tf_op jit(solution)/shard_map/reduce_scatter | solution.py:50
  60.2 24.6 %copy-start.6 = (s32[2]{0:T(128)S(1)}, s32[2]{0:T(128)}, u32[]{:S(2)}) copy-start(s32[2]{0:T(128)} %param.11) | copy-start | bytes 28
  60.3 40.1 %collective-permute-start = (bf16[128,3072]{1,0:T(8,128)(2,1)S(1)}, bf16[128,3072]{1,0:T(8,128)(2,1)}, u32[]{:S(2)}, u32[]{:S(2)}) collective-permute-start(bf16[128,3072]{1,0:T(8,128)(2,1)S(1)} %slice.102), channel_id=1, source_target_pairs={{0,8},{1,9},{2,10},{3,11},{4,12},{5,13},{6,14},{7,15},{16,24},{17,... | collective-permute-start | bytes 2359304 | tf_op jit(solution)/shard_map/ppermute | solution.py:12
  96.5 8.3 %slice-start.2 = ((s8[4718592]{0:T(1024)(128)(4,1)}), s8[4194304]{0:T(1024)(128)(4,1)S(1)}, s32[]{:S(2)}) async-start(s8[4718592]{0:T(1024)(128)(4,1)} %bitcast.59), calls=%async_computation.11 | async-start | bytes 8388608
  100.4 4.5 slice-start.3
  100.4 7.4 %slice-start.6 = ((s8[4718592]{0:T(1024)(128)(4,1)}), s8[4194304]{0:T(1024)(128)(4,1)S(1)}, s32[]{:S(2)}) async-start(s8[4718592]{0:T(1024)(128)(4,1)} %bitcast.73), calls=%async_computation.15 | async-start | bytes 8388608
  104.9 2.9 slice-start.7
  107.8 66.6 %copy-start.5 = (bf16[32,3072]{1,0:T(8,128)(2,1)S(1)}, bf16[32,3072]{1,0:T(8,128)(2,1)}, u32[]{:S(2)}) copy-start(bf16[32,3072]{1,0:T(8,128)(2,1)} %param.9) | copy-start | bytes 589828
  110.0 109.9 %all-gather.6.cloned.1.call-start = ((), (), s32[]{:S(2)}) async-start(), calls=%async_computation.5 | async-start | bytes 1769472 | tf_op jit(solution)/shard_map/all_gather | solution.py:117
  176.0 141.8 %reduce-scatter.6.cloned.1.call-start = ((), (), s32[]{:S(2)}) async-start(), calls=%async_computation.6 | async-start | bytes 1769472 | tf_op jit(solution)/shard_map/reduce_scatter | solution.py:50
  223.7 21.8 %collective-permute-start.1 = (bf16[128,3072]{1,0:T(8,128)(2,1)S(1)}, bf16[128,3072]{1,0:T(8,128)(2,1)}, u32[]{:S(2)}, u32[]{:S(2)}) collective-permute-start(bf16[128,3072]{1,0:T(8,128)(2,1)S(1)} %slice.105), channel_id=1, source_target_pairs={{0,8},{1,9},{2,10},{3,11},{4,12},{5,13},{6,14},{7,15},{16,24},{17,... | collective-permute-start | bytes 2359304 | tf_op jit(solution)/shard_map/ppermute | solution.py:12
  233.1 5.5 %slice-start = ((s8[4718592]{0:T(1024)(128)(4,1)}), s8[4194304]{0:T(1024)(128)(4,1)S(1)}, s32[]{:S(2)}) async-start(s8[4718592]{0:T(1024)(128)(4,1)} %bitcast.51), calls=%async_computation.9 | async-start | bytes 8388608
  233.1 5.5 %slice-start.1 = ((s8[4718592]{0:T(1024)(128)(4,1)}), s8[524288]{0:T(1024)(128)(4,1)S(1)}, s32[]{:S(2)}) async-start(s8[4718592]{0:T(1024)(128)(4,1)} %bitcast.51), calls=%async_computation.10 | async-start | bytes 1048576
  241.6 3.9 copy-start.1
  241.7 6.8 %slice-start.4 = ((s8[4718592]{0:T(1024)(128)(4,1)}), s8[4194304]{0:T(1024)(128)(4,1)S(1)}, s32[]{:S(2)}) async-start(s8[4718592]{0:T(1024)(128)(4,1)} %bitcast.64), calls=%async_computation.13 | async-start | bytes 8388608
  245.5 2.9 slice-start.5
  245.6 5.6 %slice-start.8 = ((s8[4718592]{0:T(1024)(128)(4,1)}), s8[4194304]{0:T(1024)(128)(4,1)S(1)}, s32[]{:S(2)}) async-start(s8[4718592]{0:T(1024)(128)(4,1)} %bitcast.75), calls=%async_computation.17 | async-start | bytes 8388608
  248.5 2.7 slice-start.9
  251.2 66.6 %copy-start.4 = (bf16[32,3072]{1,0:T(8,128)(2,1)S(1)}, bf16[32,3072]{1,0:T(8,128)(2,1)}, u32[]{:S(2)}) copy-start(bf16[32,3072]{1,0:T(8,128)(2,1)} %add_convert_fusion.2) | copy-start | bytes 589828
  251.2 68.3 %copy-start.2 = (bf16[3072,3,1,128]{3,0,2,1:T(8,128)(2,1)S(1)}, bf16[3072,3,1,128]{3,0,2,1:T(8,128)(2,1)}, u32[]{:S(2)}) copy-start(bf16[3072,3,1,128]{3,0,2,1:T(8,128)(2,1)} %param.14) | copy-start | bytes 7077892
  253.5 109.5 %all-gather.8.cloned.1.call-start = ((), (), s32[]{:S(2)}) async-start(), calls=%async_computation.7 | async-start | bytes 1769472 | tf_op jit(solution)/shard_map/all_gather | solution.py:117
  319.5 121.6 %reduce-scatter.8.cloned.1.call-start = ((), (), s32[]{:S(2)}) async-start(), calls=%async_computation.8 | async-start | bytes 1769472 | tf_op jit(solution)/shard_map/reduce_scatter | solution.py:63
  368.0 73.1 %copy-start.3 = (bf16[32,3072]{1,0:T(8,128)(2,1)S(1)}, bf16[32,3072]{1,0:T(8,128)(2,1)}, u32[]{:S(2)}) copy-start(bf16[32,3072]{1,0:T(8,128)(2,1)} %add_convert_fusion.1) | copy-start | bytes 589828
  368.2 2.7 collective-permute-start.2
  369.5 2.2 collective-permute-start.3
Sparse Core Ops, SparseCore 0:
  9.5 46.8 all-gather.3
  110.1 64.1 reduce-scatter.3
  176.8 43.1 all-gather.5
  253.6 64.1 reduce-scatter.5
  319.9 43.0 all-gather.7
  375.1 65.9 reduce-scatter.7
where the time goes:
time: 450 us
  waiting for transfers between devices  329 us (73%)
  local copies, waits for them, and re-layouts  50.2 us (11%)
  matrix products  30.3 us (7%)
  between operations  17.7 us (4%)
  other arithmetic  14.9 us (3%)
  starting transfers between devices  7.17 us (2%)
    reduce_scatter x2, waiting for transfers between devices, conv_share(): lax.psum_scatter(term(jnp.int32(0), tok_rows * lax.axis_size('head')).ast...  129 us
    all_gather x2, waiting for transfers between devices, per_device(): state = lax.all_gather(share, 'head', axis=0, tiled=True)  84.8 us
    reduce_scatter x1, waiting for transfers between devices, attention_portion_for(): lax.psum_scatter(term(jnp.int32(0), tok_rows * lax.axis_size('head')).ast...  66.2 us
    all_gather x1, waiting for transfers between devices, per_device(): state = lax.all_gather(stream, 'head', axis=0, tiled=True)  48.2 us
    unnamed x41, local copies, waits for them, and re-layouts  25.5 us
    slice x1, local copies, waits for them, and re-layouts, convolution_gate(): kernel[tap_idx].reshape(width, 2 * own_width)  22.4 us
    dot_general x6, matrix products, convolution_gate(): jnp.dot(slab, kernel[tap_idx].reshape(width, 2 * own_width), preferred_el...  20.6 us
  transfers between devices with their start and end apart: 10, of which 7 were waited for; matrix products, arithmetic and copies ran while one was open for 13% of the time, Pallas kernels for 0%

commit v1 on v0

--- a/solution.py
+++ b/solution.py
@@ -107,7 +107,15 @@
     layers = w_conv.shape[0]
     qkv_weight = w_qkv.reshape(width, 3 * head_size)
     share = stream
-    state = lax.all_gather(stream, "head", axis=0, tiled=True)
+    ways, here = (lax.axis_size("head"), lax.axis_index("head"))
+    grown, reach = (stream, 1)
+    while reach < ways:
+        theirs = lax.ppermute(grown, "head", [(d, d ^ reach) for d in range(ways)])
+        mine_first = jnp.concatenate([grown, theirs], axis=0)
+        theirs_first = jnp.concatenate([theirs, grown], axis=0)
+        grown = jnp.where(here & reach == 0, mine_first, theirs_first)
+        reach = 2 * reach
+    state = grown
     for layer_idx in range(layers):
         gated = convolution_gate(
             normed(state, gains[layer_idx]), w_conv[layer_idx], dilations[layer_idx]

time: 450 us -> 468 us (1.040)
  local copies, waits for them, and re-layouts: 50.2 us -> 61.1 us
  starting transfers between devices: 7.17 us -> 14.7 us
    all_gather x1 -> x0, waiting for transfers between devices: 48.2 us -> none  [per_device(): state = lax.all_gather(stream, 'head', axis=0, tiled=True)]
    ppermute x0 -> x3, waiting for transfers between devices: none -> 45.7 us  [per_device(): theirs = lax.ppermute(grown, 'head', [(d, d ^ reach) for d in range(ways)])]
    ppermute x0 -> x3, starting transfers between devices: none -> 7.39 us  [per_device(): theirs = lax.ppermute(grown, 'head', [(d, d ^ reach) for d in range(ways)])]
    unnamed x41 -> x43, local copies, waits for them, and re-layouts: 25.5 us -> 32.7 us
  transfers between devices with their start and end apart: 10 -> 12, of which waited for: 7 -> 9; matrix products, arithmetic and copies ran while one was open for 13% -> 15% of each run, Pallas kernels for 0% -> 0%
where the time goes in v1:
time: 468 us; the launch traced here: 467 us
  waiting for transfers between devices  328 us (70%)
  local copies, waits for them, and re-layouts  61.1 us (13%)
  matrix products  30.3 us (6%)
  between operations  17.5 us (4%)
  other arithmetic  15.2 us (3%)
  starting transfers between devices  14.7 us (3%)
    reduce_scatter x2, waiting for transfers between devices, conv_share(): lax.psum_scatter(term(jnp.int32(0), tok_rows * lax.axis_size('head')).ast...  131 us
    all_gather x2, waiting for transfers between devices, per_device(): state = lax.all_gather(share, 'head', axis=0, tiled=True)  84.8 us
    reduce_scatter x1, waiting for transfers between devices, attention_portion_for(): lax.psum_scatter(term(jnp.int32(0), tok_rows * lax.axis_size('head')).ast...  66.1 us
    ppermute x3, waiting for transfers between devices, per_device(): theirs = lax.ppermute(grown, 'head', [(d, d ^ reach) for d in range(ways)])  45.7 us
    unnamed x43, local copies, waits for them, and re-layouts  32.7 us
    slice x1, local copies, waits for them, and re-layouts, convolution_gate(): kernel[tap_idx].reshape(width, 2 * own_width)  26.1 us
    dot_general x6, matrix products, convolution_gate(): jnp.dot(slab, kernel[tap_idx].reshape(width, 2 * own_width), preferred_el...  20.6 us
  transfers between devices with their start and end apart: 12, of which 9 were waited for; matrix products, arithmetic and copies ran while one was open for 15% of the time, Pallas kernels for 0%

profile of v1, /device:TPU:0, one launch (start us, length us, event | category | flops | bytes accessed | tf_op | source)
XLA Modules:
  0.0 467.0 jit_solution(15174554862285761966)
XLA Ops:
  6.5 3.0 collective-permute-start
  9.5 5.1 %collective-permute-done = bf16[32,3072]{1,0:T(8,128)(2,1)S(1)} collective-permute-done((bf16[32,3072]{1,0:T(8,128)(2,1)}, bf16[32,3072]{1,0:T(8,128)(2,1)S(1)}, u32[]{:S(2)}, u32[]{:S(2)}) %collective-permute-start) | collective-permute-done | bytes 196640 | tf_op jit(solution)/shard_map/ppermute | solution.py:113
  14.6 1.1 maximum_select_fusion.2
  15.7 1.9 collective-permute-start.1
  17.6 8.5 %collective-permute-done.1 = bf16[64,3072]{1,0:T(8,128)(2,1)S(1)} collective-permute-done((bf16[64,3072]{1,0:T(8,128)(2,1)S(1)}, bf16[64,3072]{1,0:T(8,128)(2,1)S(1)}, u32[]{:S(2)}, u32[]{:S(2)}) %collective-permute-start.1) | collective-permute-done | bytes 393248 | tf_op jit(solution)/shard_map/ppermute | solution.py:113
  26.2 2.6 collective-permute-start.2
  28.8 0.9 fusion.93
  29.8 32.1 %collective-permute-done.2 = bf16[128,3072]{1,0:T(8,128)(2,1)S(1)} collective-permute-done((bf16[128,3072]{1,0:T(8,128)(2,1)S(1)}, bf16[128,3072]{1,0:T(8,128)(2,1)S(1)}, u32[]{:S(2)}, u32[]{:S(2)}) %collective-permute-start.2) | collective-permute-done | bytes 786464 | tf_op jit(solution)/shard_map/ppermute | solution.py:113
  61.9 0.5 fusion.5
  62.8 2.2 fusion.7
  65.0 2.2 collective-permute-start.3
  67.2 26.1 %fusion.91 = (bf16[1,1,3072,2,384]{4,3,2,1,0:T(2,128)(2,1)}, bf16[1,1,3072,2,384]{4,3,2,1,0:T(2,128)(2,1)}, bf16[1,1,3072,2,384]{4,3,2,1,0:T(2,128)(2,1)}, bf16[...) fusion(bf16[2,3,3072,2,384]{4,3,2,1,0:T(2,128)(2,1)} %param.12), kind=kLoop, calls=%fused_computation.108 | loop fusion | bytes 56623104 | tf_op jit(solution)/shard_map/slice | solution.py:38
  93.4 0.7 fusion.94
  96.0 5.4 %copy.10 = bf16[384,8,2,384]{3,1,2,0:T(8,128)(2,1)} copy(bf16[384,8,2,384]{3,2,1,0:T(2,128)(2,1)} %bitcast.58) | data formatting | bytes 9437184
  101.4 3.0 copy.9
  104.5 5.3 %copy.11 = bf16[384,8,2,384]{3,1,2,0:T(8,128)(2,1)} copy(bf16[384,8,2,384]{3,2,1,0:T(2,128)(2,1)} %bitcast.54) | data formatting | bytes 9437184
  109.8 3.9 fusion.96
  113.7 3.0 fusion.28
  116.7 2.9 add_add_fusion
  119.7 2.2 convolution_convert_fusion.2
  122.0 66.4 %reduce-scatter.4.cloned.1.call-done = bf16[32,3072]{1,0:T(8,128)(2,1)} async-done(((bf16[256,3072]{1,0:T(8,128)(2,1)}), bf16[32,3072]{1,0:T(8,128)(2,1)}) %reduce-scatter.4.cloned.1.call-update) | async-done | bytes 196624 | tf_op jit(solution)/shard_map/reduce_scatter | solution.py:50
  188.4 1.6 add_convert_fusion.2
  190.2 43.8 %all-gather.3.cloned.1.call-done = bf16[256,3072]{1,0:T(8,128)(2,1)} async-done(((bf16[32,3072]{1,0:T(8,128)(2,1)}), bf16[256,3072]{1,0:T(8,128)(2,1)}) %all-gather.3.cloned.1.call-update) | async-done | bytes 1572880 | tf_op jit(solution)/shard_map/all_gather | solution.py:125
  234.0 1.8 fusion.8
  235.8 1.9 fusion.10
  237.8 2.2 collective-permute-start.4
  242.0 5.3 %copy.12 = bf16[384,8,2,384]{3,1,2,0:T(8,128)(2,1)} copy(bf16[384,8,2,384]{3,2,1,0:T(2,128)(2,1)} %bitcast.53) | data formatting | bytes 9437184
  247.3 5.4 %copy.14 = bf16[384,8,2,384]{3,1,2,0:T(8,128)(2,1)} copy(bf16[384,8,2,384]{3,2,1,0:T(2,128)(2,1)} %bitcast.52) | data formatting | bytes 9437184
  252.7 5.3 %copy.13 = bf16[384,8,2,384]{3,1,2,0:T(8,128)(2,1)} copy(bf16[384,8,2,384]{3,2,1,0:T(2,128)(2,1)} %bitcast.51) | data formatting | bytes 9437184
  258.0 3.9 fusion.97
  261.9 4.2 fusion.19
  266.2 2.7 fusion.37
  268.9 2.2 convolution_convert_fusion.1
  271.2 64.2 %reduce-scatter.6.cloned.1.call-done = bf16[32,3072]{1,0:T(8,128)(2,1)} async-done(((bf16[256,3072]{1,0:T(8,128)(2,1)}), bf16[32,3072]{1,0:T(8,128)(2,1)}) %reduce-scatter.6.cloned.1.call-update) | async-done | bytes 196624 | tf_op jit(solution)/shard_map/reduce_scatter | solution.py:50
  335.5 1.6 add_convert_fusion.1
  337.2 2.5 copy.8
  339.7 41.0 %all-gather.5.cloned.1.call-done = bf16[256,3072]{1,0:T(8,128)(2,1)} async-done(((bf16[32,3072]{1,0:T(8,128)(2,1)}), bf16[256,3072]{1,0:T(8,128)(2,1)}) %all-gather.5.cloned.1.call-update) | async-done | bytes 1572880 | tf_op jit(solution)/shard_map/all_gather | solution.py:125
  380.7 1.8 fusion.11
  382.5 3.2 fusion.40
  385.9 1.4 collective-permute-start.5
  387.4 1.3 collective-permute-start.6
  388.7 0.8 collective-permute-done.6
  389.5 0.6 conditional.1
  389.6 0.6 broadcast.54
  390.1 0.7 multiply_add_fusion
  390.8 1.9 convolution_convert_fusion
  392.8 66.1 %reduce-scatter.8.cloned.1.call-done = bf16[32,3072]{1,0:T(8,128)(2,1)} async-done(((bf16[256,3072]{1,0:T(8,128)(2,1)}), bf16[32,3072]{1,0:T(8,128)(2,1)}) %reduce-scatter.8.cloned.1.call-update) | async-done | bytes 196624 | tf_op jit(solution)/shard_map/reduce_scatter | solution.py:63
  458.8 1.6 add_convert_fusion
  (65 shorter events, 1.3 us)
Async XLA Ops:
  6.5 384.3 %copy-start = (bf16[1,128,3072]{2,1,0:T(8,128)(2,1)S(1)}, bf16[1,128,3072]{2,1,0:T(8,128)(2,1)}, u32[]{:S(2)}) copy-start(bf16[1,128,3072]{2,1,0:T(8,128)(2,1)} %param.15) | copy-start | bytes 2359300
  6.5 181.9 %reduce-scatter.4.cloned.1.call-start = ((), (), s32[]{:S(2)}) async-start(), calls=%async_computation.3 | async-start | bytes 1769472 | tf_op jit(solution)/shard_map/reduce_scatter | solution.py:50
  6.5 8.1 %collective-permute-start = (bf16[32,3072]{1,0:T(8,128)(2,1)}, bf16[32,3072]{1,0:T(8,128)(2,1)S(1)}, u32[]{:S(2)}, u32[]{:S(2)}) collective-permute-start(bf16[32,3072]{1,0:T(8,128)(2,1)} %param.9), channel_id=1, source_target_pairs={{0,1},{1,0},{2,3},{3,2},{4,5},{5,4},{6,7},{7,6},{8,9},{9,8},{10,11... | collective-permute-start | bytes 589832 | tf_op jit(solution)/shard_map/ppermute | solution.py:113
  15.7 10.4 %collective-permute-start.1 = (bf16[64,3072]{1,0:T(8,128)(2,1)S(1)}, bf16[64,3072]{1,0:T(8,128)(2,1)S(1)}, u32[]{:S(2)}, u32[]{:S(2)}) collective-permute-start(bf16[64,3072]{1,0:T(8,128)(2,1)S(1)} %maximum_select_fusion.2), channel_id=1, source_target_pairs={{0,2},{1,3},{2,0},{3,1},{4,6},{5,7},{6,4},{7,5},{8,10},{9,11},{10,... | collective-permute-start | bytes 1179656 | tf_op jit(solution)/shard_map/ppermute | solution.py:113
  26.2 35.6 %collective-permute-start.2 = (bf16[128,3072]{1,0:T(8,128)(2,1)S(1)}, bf16[128,3072]{1,0:T(8,128)(2,1)S(1)}, u32[]{:S(2)}, u32[]{:S(2)}) collective-permute-start(bf16[128,3072]{1,0:T(8,128)(2,1)S(1)} %maximum_select_fusion.1), channel_id=1, source_target_pairs={{0,4},{1,5},{2,6},{3,7},{4,0},{5,1},{6,2},{7,3},{8,12},{9,13},{10,... | collective-permute-start | bytes 2359304 | tf_op jit(solution)/shard_map/ppermute | solution.py:113
  61.9 0.9 copy-start.2
  65.0 28.3 %copy-start.7 = (s32[2]{0:T(128)S(1)}, s32[2]{0:T(128)}, u32[]{:S(2)}) copy-start(s32[2]{0:T(128)} %param.11) | copy-start | bytes 28
  65.0 48.6 %collective-permute-start.3 = (bf16[128,3072]{1,0:T(8,128)(2,1)S(1)}, bf16[128,3072]{1,0:T(8,128)(2,1)}, u32[]{:S(2)}, u32[]{:S(2)}) collective-permute-start(bf16[128,3072]{1,0:T(8,128)(2,1)S(1)} %slice.102), channel_id=1, source_target_pairs={{0,8},{1,9},{2,10},{3,11},{4,12},{5,13},{6,14},{7,15},{16,24},{17,... | collective-permute-start | bytes 2359304 | tf_op jit(solution)/shard_map/ppermute | solution.py:12
  96.0 5.4 %slice-start = ((s8[4718592]{0:T(1024)(128)(4,1)}), s8[4194304]{0:T(1024)(128)(4,1)S(1)}, s32[]{:S(2)}) async-start(s8[4718592]{0:T(1024)(128)(4,1)} %bitcast.55), calls=%async_computation.8 | async-start | bytes 8388608
  96.0 5.4 %slice-start.1 = ((s8[4718592]{0:T(1024)(128)(4,1)}), s8[524288]{0:T(1024)(128)(4,1)S(1)}, s32[]{:S(2)}) async-start(s8[4718592]{0:T(1024)(128)(4,1)} %bitcast.55), calls=%async_computation.9 | async-start | bytes 1048576
  109.8 3.9 copy-start.1
  109.8 6.9 %slice-start.2 = ((s8[4718592]{0:T(1024)(128)(4,1)}), s8[4194304]{0:T(1024)(128)(4,1)S(1)}, s32[]{:S(2)}) async-start(s8[4718592]{0:T(1024)(128)(4,1)} %bitcast.60), calls=%async_computation.10 | async-start | bytes 8388608
  113.7 3.0 slice-start.3
  113.7 6.0 %slice-start.6 = ((s8[4718592]{0:T(1024)(128)(4,1)}), s8[4194304]{0:T(1024)(128)(4,1)S(1)}, s32[]{:S(2)}) async-start(s8[4718592]{0:T(1024)(128)(4,1)} %bitcast.73), calls=%async_computation.14 | async-start | bytes 8388608
  116.7 3.0 slice-start.7
  119.7 68.7 %copy-start.6 = (bf16[32,3072]{1,0:T(8,128)(2,1)S(1)}, bf16[32,3072]{1,0:T(8,128)(2,1)}, u32[]{:S(2)}) copy-start(bf16[32,3072]{1,0:T(8,128)(2,1)} %param.9) | copy-start | bytes 589828
  122.0 112.0 %all-gather.3.cloned.1.call-start = ((), (), s32[]{:S(2)}) async-start(), calls=%async_computation.4 | async-start | bytes 1769472 | tf_op jit(solution)/shard_map/all_gather | solution.py:125
  190.1 145.4 %reduce-scatter.6.cloned.1.call-start = ((), (), s32[]{:S(2)}) async-start(), calls=%async_computation.5 | async-start | bytes 1769472 | tf_op jit(solution)/shard_map/reduce_scatter | solution.py:50
  237.8 24.1 %collective-permute-start.4 = (bf16[128,3072]{1,0:T(8,128)(2,1)S(1)}, bf16[128,3072]{1,0:T(8,128)(2,1)}, u32[]{:S(2)}, u32[]{:S(2)}) collective-permute-start(bf16[128,3072]{1,0:T(8,128)(2,1)S(1)} %slice.105), channel_id=1, source_target_pairs={{0,8},{1,9},{2,10},{3,11},{4,12},{5,13},{6,14},{7,15},{16,24},{17,... | collective-permute-start | bytes 2359304 | tf_op jit(solution)/shard_map/ppermute | solution.py:12
  258.0 8.2 %slice-start.4 = ((s8[4718592]{0:T(1024)(128)(4,1)}), s8[4194304]{0:T(1024)(128)(4,1)S(1)}, s32[]{:S(2)}) async-start(s8[4718592]{0:T(1024)(128)(4,1)} %bitcast.63), calls=%async_computation.12 | async-start | bytes 8388608
  261.9 4.3 slice-start.5
  261.9 7.0 %slice-start.8 = ((s8[4718592]{0:T(1024)(128)(4,1)}), s8[4194304]{0:T(1024)(128)(4,1)S(1)}, s32[]{:S(2)}) async-start(s8[4718592]{0:T(1024)(128)(4,1)} %bitcast.75), calls=%async_computation.16 | async-start | bytes 8388608
  266.2 2.7 slice-start.9
  268.9 66.6 %copy-start.5 = (bf16[32,3072]{1,0:T(8,128)(2,1)S(1)}, bf16[32,3072]{1,0:T(8,128)(2,1)}, u32[]{:S(2)}) copy-start(bf16[32,3072]{1,0:T(8,128)(2,1)} %add_convert_fusion.2) | copy-start | bytes 589828
  268.9 68.3 %copy-start.3 = (bf16[3072,3,1,128]{3,0,2,1:T(8,128)(2,1)S(1)}, bf16[3072,3,1,128]{3,0,2,1:T(8,128)(2,1)}, u32[]{:S(2)}) copy-start(bf16[3072,3,1,128]{3,0,2,1:T(8,128)(2,1)} %param.14) | copy-start | bytes 7077892
  271.2 109.5 %all-gather.5.cloned.1.call-start = ((), (), s32[]{:S(2)}) async-start(), calls=%async_computation.6 | async-start | bytes 1769472 | tf_op jit(solution)/shard_map/all_gather | solution.py:125
  337.1 121.7 %reduce-scatter.8.cloned.1.call-start = ((), (), s32[]{:S(2)}) async-start(), calls=%async_computation.7 | async-start | bytes 1769472 | tf_op jit(solution)/shard_map/reduce_scatter | solution.py:63
  385.9 72.9 %copy-start.4 = (bf16[32,3072]{1,0:T(8,128)(2,1)S(1)}, bf16[32,3072]{1,0:T(8,128)(2,1)}, u32[]{:S(2)}) copy-start(bf16[32,3072]{1,0:T(8,128)(2,1)} %add_convert_fusion.1) | copy-start | bytes 589828
  385.9 2.8 collective-permute-start.5
  387.4 2.2 collective-permute-start.6
Sparse Core Ops, SparseCore 0:
  122.1 66.2 reduce-scatter.3
  190.8 43.1 all-gather.2
  271.3 64.1 reduce-scatter.5
  337.5 43.1 all-gather.4
  392.9 65.9 reduce-scatter.7
